TPU v7x, 32 devices: a whole 2x2x4 slice. The times are simulated.
32 devices in a mesh: row: 4 (over x, core), col: 8 (over z, y).
Axes of the slice: x: 2, y: 2, z: 4, core: 2. Of those that a mesh axis runs over, the one named last changes fastest.
Arguments:
- right_side: float32 [64, 16384], P(None, 'row'), may hold values from -8 to 8
- blocks: bfloat16 [3072, 128, 128], P(('row', 'col')), may hold values from -1 to 1
- targets: int32 [3072, 1], P(('row', 'col')), may hold values from 0 to 7; in each aligned block of 96 rows (0 to 95, 96 to 191, ...) at most 24 rows name the same one
- tile_rows: int32 [3072], P(('row', 'col')), may hold values from 0 to 31
- tile_cols: int32 [3072], P(('row', 'col')), may hold values from 0 to 31
Outputs:
- solution: float32 [64, 8, 4096], P(None, 'col', 'row')
- phibar: float32 [64], replicated
Inputs may be any that keep to these rules, and one draw needn't show every extreme that they name: `targets`: among the 96 blocks of one device, at most 24 name the same grid column, and some grid column is named exactly 24 times by some device.
All inputs are finite; a program needn't handle non-finite values.
Results may differ from a plain program's by a relative error of at most 0.0032.
Values may be sent and summed in bfloat16 or wider, within the bound.
No kernel may reach another device: no remote copies, remote signals or barrier semaphores. Data moves between devices by JAX's collectives and lax.ppermute only.
A program may use at most 128 MiB of HBM per device.

v0:
```python
import jax
import jax.numpy as jnp
from jax import lax
from jax.sharding import PartitionSpec as P

TC = 32
ITERS = 4
EPSILON = 1e-06


def gather_tiles(vector_bf, indices, block_size):
    snapshots, extent = vector_bf.shape
    vector_tiles = vector_bf.reshape(snapshots, extent // block_size, block_size)
    return jnp.take(vector_tiles, indices, axis=1)


def place_terms(weighted, indices, n_out):
    snapshots, number, block_size = weighted.shape
    onehot = (indices[:, None] == jnp.arange(n_out, dtype=jnp.int32)[None, :]).astype(jnp.float32)
    summed = jnp.einsum("ksi,st->kti", weighted, onehot, precision=lax.Precision.HIGHEST)
    return summed.reshape(snapshots, n_out * block_size)


def forward_terms(vector_bf, blocks, row_index, col_index, n_out):
    picked = gather_tiles(vector_bf, col_index, blocks.shape[1])
    weighted = jnp.einsum("sij,ksj->ksi", blocks, picked, preferred_element_type=jnp.float32)
    return place_terms(weighted, row_index, n_out)


def backward_terms(vector_bf, blocks, row_index, col_index, n_out):
    picked = gather_tiles(vector_bf, row_index, blocks.shape[1])
    weighted = jnp.einsum("sji,ksj->ksi", blocks, picked, preferred_element_type=jnp.float32)
    return place_terms(weighted, col_index, n_out)


def per_device(right_side, blocks, targets, tile_rows, tile_cols):
    col_count = lax.axis_size("col")
    row_count = lax.axis_size("row")
    block_size = blocks.shape[1]
    snapshots = right_side.shape[0]
    row_tiles = right_side.shape[1] // block_size
    own_count = blocks.shape[0]
    capacity = 2 * own_count // col_count
    target = targets[:, 0]
    matches = (target[:, None] == jnp.arange(col_count, dtype=jnp.int32)[None, :]).astype(jnp.int32)
    before = jnp.cumsum(matches, axis=0) - matches
    slot_index = target * capacity + jnp.sum(before * matches, axis=1)
    outgoing = (
        jnp.zeros((col_count * capacity, block_size, block_size), blocks.dtype)
        .at[slot_index]
        .set(blocks)
    )
    places = (
        jnp.zeros((col_count * capacity, 2), jnp.int32)
        .at[slot_index]
        .set(jnp.stack([tile_rows, tile_cols], axis=1))
    )
    arrived, arrived_places = (
        lax.all_to_all(
            outgoing.reshape(col_count, capacity, block_size, block_size),
            "col",
            split_axis=0,
            concat_axis=0,
            tiled=True,
        ),
        lax.all_to_all(
            places.reshape(col_count, capacity, 2), "col", split_axis=0, concat_axis=0, tiled=True
        ),
    )
    work_blocks = arrived.reshape(col_count * capacity, block_size, block_size)
    flat_places = arrived_places.reshape(col_count * capacity, 2)
    work_rows = flat_places[:, 0]
    work_cols = flat_places[:, 1]

    def backward(left_bf):
        return backward_terms(left_bf, work_blocks, work_rows, work_cols, TC)

    def sum_right(partial_value):
        return lax.psum(partial_value, "row")

    def finish_left(unscaled, need_form):
        squares = jnp.sum(unscaled * unscaled, axis=1)
        total = lax.psum(squares, "row")
        beta_norm = jnp.sqrt(total + EPSILON)
        scaled = unscaled / beta_norm[:, None]
        rounded = None
        if need_form:
            rounded = scaled.astype(jnp.bfloat16)
        return (beta_norm, scaled, rounded)

    def finish_right(unscaled):
        squares = jnp.sum(unscaled * unscaled, axis=1)
        total = lax.psum(squares, "col")
        alpha_norm = jnp.sqrt(total + EPSILON)
        scaled = unscaled / alpha_norm[:, None]
        rounded = scaled.astype(jnp.bfloat16)
        return (alpha_norm, scaled, rounded)

    beta_norm, left_vec, left_bf = finish_left(right_side, True)
    alpha_norm, right_vec, right_bf = finish_right(sum_right(backward(left_bf)))
    search = right_vec
    solution = jnp.zeros_like(right_vec)
    phibar = beta_norm
    rhobar = alpha_norm
    for iteration in range(ITERS):
        last_turn = iteration + 1 == ITERS
        unscaled = (
            lax.psum(forward_terms(right_bf, work_blocks, work_rows, work_cols, row_tiles), "col")
            - alpha_norm[:, None] * left_vec
        )
        beta_norm, left_vec, left_bf = finish_left(unscaled, not last_turn)
        rho_value = jnp.sqrt(rhobar * rhobar + beta_norm * beta_norm)
        cosine = rhobar / rho_value
        sine_value = beta_norm / rho_value
        phi_value = cosine * phibar
        phibar = sine_value * phibar
        solution = solution + (phi_value / rho_value)[:, None] * search
        if not last_turn:
            unscaled = sum_right(backward(left_bf)) - beta_norm[:, None] * right_vec
            alpha_norm, right_vec, right_bf = finish_right(unscaled)
            theta_value = sine_value * alpha_norm
            rhobar = -cosine * alpha_norm
            search = right_vec - (theta_value / rho_value)[:, None] * search
    share_len = solution.shape[1] // row_count
    solution = lax.dynamic_slice_in_dim(solution, lax.axis_index("row") * share_len, share_len, 1)
    return (solution.reshape(snapshots, 1, solution.shape[1]), phibar)


def solution(mesh):
    placed = (
        P(None, "row"),
        P(("row", "col"), None, None),
        P(("row", "col"), None),
        P(("row", "col")),
        P(("row", "col")),
    )
    return jax.shard_map(
        per_device,
        mesh=mesh,
        in_specs=placed,
        out_specs=(P(None, "col", "row"), P()),
        check_vma=False,
    )
```

profile of v0, /device:TPU:0, one launch (start us, length us, event | category | flops | bytes accessed | tf_op | source)
XLA Modules:
  0.0 906.9 jit_solution(17280355181446882380)
XLA Ops:
  11.9 7.3 all-to-all-start
  19.2 4.2 broadcast_in_dim.14
  23.4 14.7 %scatter_fusion = bf16[192,128,128]{2,1,0:T(8,128)(2,1)} fusion(bf16[192,128,128]{2,1,0:T(8,128)(2,1)} %broadcast_in_dim.14, s32[96]{0:T(128)S(1)} %fusion.105, bf16[96,128,128]{2,1,0:T(8,128)(2,1)} %param.8), kind=kCustom, calls=%fused_computation.9 | custom fusion | bytes 9437568 | tf_op jit(solution)/shard_map/scatter | solution.py:51
  38.1 6.1 all-to-all-start.1
  44.4 5.7 psum.119
  50.5 2.7 gather_fusion
  53.3 128.6 %all-to-all-done.1 = bf16[8,24,128,128]{3,2,1,0:T(8,128)(2,1)} async-done(((bf16[8,24,128,128]{3,2,1,0:T(8,128)(2,1)}), bf16[8,24,128,128]{3,2,1,0:T(8,128)(2,1)}, u32[]{:S(2)}, u32[]{:S(2)}) %all-to-all-start.1) | async-done | bytes 6291488 | tf_op jit(solution)/shard_map/all_to_all | solution.py:59
  181.9 5.6 fusion.48
  187.5 5.7 fusion.14
  194.9 35.2 %all-reduce.9.cloned.1.call-done = f32[64,4096]{1,0:T(8,128)} async-done(((f32[64,4096]{1,0:T(8,128)}), f32[64,4096]{1,0:T(8,128)}) %all-reduce.9.cloned.1.call-update) | async-done | bytes 1048592 | tf_op jit(solution)/shard_map/psum | solution.py:79
  231.5 21.5 %psum.121 = f32[64]{0:T(128)S(1)} all-reduce(f32[64]{0:T(128)S(1)} %multiply_reduce_fusion.7), channel_id=1, replica_groups=mesh['row'=4,'col'=8] {'col'}, use_global_device_ids=true, to_apply=%region_8.10 | all-reduce | flops 64 | bytes 512 | tf_op jit(solution)/shard_map/psum | solution.py:93
  254.6 2.8 gather_fusion.1
  257.4 8.1 fusion.51
  265.4 5.7 fusion.12
  272.8 75.0 %all-reduce.11.cloned.1.call-done = f32[64,4096]{1,0:T(8,128)} async-done(((f32[64,4096]{1,0:T(8,128)}), f32[64,4096]{1,0:T(8,128)}) %all-reduce.11.cloned.1.call-update) | async-done | bytes 1048592 | tf_op jit(solution)/shard_map/psum | solution.py:108
  350.4 6.1 psum.123
  357.9 2.8 gather_fusion.2
  360.7 5.6 fusion.54
  366.3 5.7 fusion.10
  373.7 35.8 %all-reduce.13.cloned.1.call-done = f32[64,4096]{1,0:T(8,128)} async-done(((f32[64,4096]{1,0:T(8,128)}), f32[64,4096]{1,0:T(8,128)}) %all-reduce.13.cloned.1.call-update) | async-done | bytes 1048592 | tf_op jit(solution)/shard_map/psum | solution.py:79
  411.0 21.8 %psum.125 = f32[64]{0:T(128)S(1)} all-reduce(f32[64]{0:T(128)S(1)} %multiply_reduce_fusion.5), channel_id=1, replica_groups=mesh['row'=4,'col'=8] {'col'}, use_global_device_ids=true, to_apply=%region_14.16 | all-reduce | flops 64 | bytes 512 | tf_op jit(solution)/shard_map/psum | solution.py:93
  434.5 2.8 gather_fusion.3
  437.2 8.1 fusion.57
  445.3 5.8 fusion.8
  452.8 75.0 %all-reduce.15.cloned.1.call-done = f32[64,4096]{1,0:T(8,128)} async-done(((f32[64,4096]{1,0:T(8,128)}), f32[64,4096]{1,0:T(8,128)}) %all-reduce.15.cloned.1.call-update) | async-done | bytes 1048592 | tf_op jit(solution)/shard_map/psum | solution.py:108
  527.8 2.6 multiply_reduce_fusion.4
  530.3 6.1 psum.127
  537.8 2.8 gather_fusion.4
  540.6 5.6 fusion.60
  546.1 5.8 fusion.6
  553.6 35.8 %all-reduce.17.cloned.1.call-done = f32[64,4096]{1,0:T(8,128)} async-done(((f32[64,4096]{1,0:T(8,128)}), f32[64,4096]{1,0:T(8,128)}) %all-reduce.17.cloned.1.call-update) | async-done | bytes 1048592 | tf_op jit(solution)/shard_map/psum | solution.py:79
  591.0 21.6 %psum.129 = f32[64]{0:T(128)S(1)} all-reduce(f32[64]{0:T(128)S(1)} %multiply_reduce_fusion.3), channel_id=1, replica_groups=mesh['row'=4,'col'=8] {'col'}, use_global_device_ids=true, to_apply=%region_20.22 | all-reduce | flops 64 | bytes 512 | tf_op jit(solution)/shard_map/psum | solution.py:93
  615.1 2.8 gather_fusion.5
  617.9 8.1 fusion.63
  626.0 5.8 fusion.4
  633.5 75.0 %all-reduce.19.cloned.1.call-done = f32[64,4096]{1,0:T(8,128)} async-done(((f32[64,4096]{1,0:T(8,128)}), f32[64,4096]{1,0:T(8,128)}) %all-reduce.19.cloned.1.call-update) | async-done | bytes 1048592 | tf_op jit(solution)/shard_map/psum | solution.py:108
  708.5 2.6 multiply_reduce_fusion.2
  711.0 6.3 psum.131
  718.7 2.8 gather_fusion.6
  721.5 5.6 fusion.66
  727.1 5.8 fusion.2
  734.5 35.8 %all-reduce.21.cloned.1.call-done = f32[64,4096]{1,0:T(8,128)} async-done(((f32[64,4096]{1,0:T(8,128)}), f32[64,4096]{1,0:T(8,128)}) %all-reduce.21.cloned.1.call-update) | async-done | bytes 1048592 | tf_op jit(solution)/shard_map/psum | solution.py:79
  771.9 21.5 %psum.133 = f32[64]{0:T(128)S(1)} all-reduce(f32[64]{0:T(128)S(1)} %multiply_reduce_fusion.1), channel_id=1, replica_groups=mesh['row'=4,'col'=8] {'col'}, use_global_device_ids=true, to_apply=%region_26.28 | all-reduce | flops 64 | bytes 512 | tf_op jit(solution)/shard_map/psum | solution.py:93
  796.0 2.8 gather_fusion.7
  798.8 8.1 fusion.69
  806.9 5.8 fusion
  814.4 75.1 %all-reduce.23.cloned.1.call-done = f32[64,4096]{1,0:T(8,128)} async-done(((f32[64,4096]{1,0:T(8,128)}), f32[64,4096]{1,0:T(8,128)}) %all-reduce.23.cloned.1.call-update) | async-done | bytes 1048592 | tf_op jit(solution)/shard_map/psum | solution.py:108
  891.0 5.9 psum.135
  (84 shorter events, 44.2 us)
Async XLA Ops:
  11.9 26.2 %all-to-all-start = ((s32[8,24,2]{1,2,0:T(2,128)}), s32[8,24,2]{1,2,0:T(2,128)S(1)}, u32[]{:S(2)}, u32[]{:S(2)}) async-start(s32[8,24,2]{1,2,0:T(2,128)} %copy.46), calls=%async_computation | async-start | bytes 16384 | tf_op jit(solution)/shard_map/all_to_all | solution.py:66
  38.1 6.1 copy-start.1
  38.1 143.8 %all-to-all-start.1 = ((bf16[8,24,128,128]{3,2,1,0:T(8,128)(2,1)}), bf16[8,24,128,128]{3,2,1,0:T(8,128)(2,1)}, u32[]{:S(2)}, u32[]{:S(2)}) async-start(bf16[8,24,128,128]{3,2,1,0:T(8,128)(2,1)} %bitcast.172), calls=%async_computation.1 | async-start | bytes 12582912 | tf_op jit(solution)/shard_map/all_to_all | solution.py:59
  44.2 185.9 %all-reduce.9.cloned.1.call-start = ((), (), s32[]{:S(2)}) async-start(), calls=%async_computation.2 | async-start | bytes 2097152 | tf_op jit(solution)/shard_map/psum | solution.py:79
  194.8 153.0 %all-reduce.11.cloned.1.call-start = ((), (), s32[]{:S(2)}) async-start(), calls=%async_computation.3 | async-start | bytes 2097152 | tf_op jit(solution)/shard_map/psum | solution.py:108
  272.8 136.7 %all-reduce.13.cloned.1.call-start = ((), (), s32[]{:S(2)}) async-start(), calls=%async_computation.4 | async-start | bytes 2097152 | tf_op jit(solution)/shard_map/psum | solution.py:79
  373.6 154.1 %all-reduce.15.cloned.1.call-start = ((), (), s32[]{:S(2)}) async-start(), calls=%async_computation.5 | async-start | bytes 2097152 | tf_op jit(solution)/shard_map/psum | solution.py:108
  451.1 76.6 %copy-start.4 = (f32[64,4096]{1,0:T(8,128)S(1)}, f32[64,4096]{1,0:T(8,128)}, u32[]{:S(2)}) copy-start(f32[64,4096]{1,0:T(8,128)} %get-tuple-element.25) | copy-start | bytes 3145732
  452.7 136.7 %all-reduce.17.cloned.1.call-start = ((), (), s32[]{:S(2)}) async-start(), calls=%async_computation.6 | async-start | bytes 2097152 | tf_op jit(solution)/shard_map/psum | solution.py:79
  553.5 154.9 %all-reduce.19.cloned.1.call-start = ((), (), s32[]{:S(2)}) async-start(), calls=%async_computation.7 | async-start | bytes 2097152 | tf_op jit(solution)/shard_map/psum | solution.py:108
  631.8 76.6 %copy-start.3 = (f32[64,4096]{1,0:T(8,128)S(1)}, f32[64,4096]{1,0:T(8,128)}, u32[]{:S(2)}) copy-start(f32[64,4096]{1,0:T(8,128)} %get-tuple-element.21) | copy-start | bytes 3145732
  633.4 136.9 %all-reduce.21.cloned.1.call-start = ((), (), s32[]{:S(2)}) async-start(), calls=%async_computation.8 | async-start | bytes 2097152 | tf_op jit(solution)/shard_map/psum | solution.py:79
  732.9 37.5 %copy-start = (f32[64,4096]{1,0:T(8,128)S(1)}, f32[64,4096]{1,0:T(8,128)}, u32[]{:S(2)}) copy-start(f32[64,4096]{1,0:T(8,128)} %get-tuple-element.19) | copy-start | bytes 3145732
  734.5 155.0 %all-reduce.23.cloned.1.call-start = ((), (), s32[]{:S(2)}) async-start(), calls=%async_computation.9 | async-start | bytes 2097152 | tf_op jit(solution)/shard_map/psum | solution.py:108
  812.7 76.8 %copy-start.2 = (f32[64,4096]{1,0:T(8,128)S(1)}, f32[64,4096]{1,0:T(8,128)}, u32[]{:S(2)}) copy-start(f32[64,4096]{1,0:T(8,128)} %get-tuple-element.17) | copy-start | bytes 3145732
Sparse Core Ops, SparseCore 0:
  194.9 35.0 all-reduce.8
  272.9 74.8 all-reduce.10
  373.7 35.7 all-reduce.12
  452.9 74.8 all-reduce.14
  553.7 35.7 all-reduce.16
  633.5 74.8 all-reduce.18
  734.6 35.7 all-reduce.20
  814.5 74.9 all-reduce.22
where the time goes:
time: 916 us; the launch traced here: 907 us
  waiting for transfers between devices  571 us (62%)
  blocking collectives  116 us (13%)
  matrix products  101 us (11%)
  local copies, waits for them, and re-layouts  56.9 us (6%)
  other arithmetic  32.9 us (4%)
  between operations  14.7 us (2%)
  starting transfers between devices  13.7 us (1%)
    psum x4, waiting for transfers between devices, per_device(): lax.psum(forward_terms(right_bf, work_blocks, work_rows, work_cols, row_t...  300 us
    psum x4, waiting for transfers between devices, sum_right(): return lax.psum(partial_value, 'row')  143 us
    all_to_all x1, waiting for transfers between devices, per_device(): lax.all_to_all(outgoing.reshape(col_count, capacity, block_size, block_si...  129 us
    psum x4, blocking collectives, finish_right(): total = lax.psum(squares, 'col')  86.4 us
    dot_general x8, matrix products, place_terms(): jnp.einsum('ksi,st->kti', weighted, onehot, precision=lax.Precision.HIGHEST)  46.2 us
    dot_general x4, matrix products, forward_terms(): jnp.einsum('sij,ksj->ksi', blocks, picked, preferred_element_type=jnp.flo...  32.3 us
    psum x5, blocking collectives, finish_left(): total = lax.psum(squares, 'row')  30.1 us
    dot_general x4, matrix products, backward_terms(): jnp.einsum('sji,ksj->ksi', blocks, picked, preferred_element_type=jnp.flo...  22.3 us
  transfers between devices with their start and end apart: 10, of which 9 were waited for; matrix products, arithmetic and copies ran while one was open for 2% of the time, Pallas kernels for 0%

commit v1 on v0

--- a/solution.py
+++ b/solution.py
@@ -105,7 +105,12 @@
     for iteration in range(ITERS):
         last_turn = iteration + 1 == ITERS
         unscaled = (
-            lax.psum(forward_terms(right_bf, work_blocks, work_rows, work_cols, row_tiles), "col")
+            jnp.sum(
+                lax.all_gather(
+                    forward_terms(right_bf, work_blocks, work_rows, work_cols, row_tiles), "col"
+                ),
+                axis=0,
+            )
             - alpha_norm[:, None] * left_vec
         )
         beta_norm, left_vec, left_bf = finish_left(unscaled, not last_turn)

time: 916 us -> 1120 us (1.22)
  waiting for transfers between devices: 571 us -> 754 us
  other arithmetic: 32.9 us -> 52.9 us
    all_gather x0 -> x4, waiting for transfers between devices: none -> 487 us  [per_device(): lax.all_gather(forward_terms(right_bf, work_blocks, work_rows, work_cols,...]
    psum x4 -> x0, waiting for transfers between devices: 300 us -> none  [per_device(): lax.psum(forward_terms(right_bf, work_blocks, work_rows, work_cols, row_t...]
    reduce_sum x0 -> x4, other arithmetic: none -> 19.9 us  [per_device(): jnp.sum(lax.all_gather(forward_terms(right_bf, work_blocks, work_rows, wo...]
where the time goes in v1:
time: 1120 us; the launch traced here: 1110 us
  waiting for transfers between devices  754 us (67%)
  blocking collectives  118 us (11%)
  matrix products  102 us (9%)
  local copies, waits for them, and re-layouts  56.4 us (5%)
  other arithmetic  52.9 us (5%)
  between operations  14.7 us (1%)
  starting transfers between devices  13.8 us (1%)
    all_gather x4, waiting for transfers between devices, per_device(): lax.all_gather(forward_terms(right_bf, work_blocks, work_rows, work_cols,...  487 us
    psum x4, waiting for transfers between devices, sum_right(): return lax.psum(partial_value, 'row')  138 us
    all_to_all x1, waiting for transfers between devices, per_device(): lax.all_to_all(outgoing.reshape(col_count, capacity, block_size, block_si...  129 us
    psum x4, blocking collectives, finish_right(): total = lax.psum(squares, 'col')  86.4 us
    dot_general x8, matrix products, place_terms(): jnp.einsum('ksi,st->kti', weighted, onehot, precision=lax.Precision.HIGHEST)  47 us
    dot_general x4, matrix products, forward_terms(): jnp.einsum('sij,ksj->ksi', blocks, picked, preferred_element_type=jnp.flo...  32.3 us
    psum x5, blocking collectives, finish_left(): total = lax.psum(squares, 'row')  31.1 us
  transfers between devices with their start and end apart: 10, of which 9 were waited for; matrix products, arithmetic and copies ran while one was open for 2% of the time, Pallas kernels for 0%

profile of v1, /device:TPU:0, one launch (start us, length us, event | category | flops | bytes accessed | tf_op | source)
XLA Modules:
  0.0 1110.3 jit_solution(16508610900727394507)
XLA Ops:
  11.9 7.3 all-to-all-start
  19.2 4.2 broadcast_in_dim.14
  23.4 14.7 %scatter_fusion = bf16[192,128,128]{2,1,0:T(8,128)(2,1)} fusion(bf16[192,128,128]{2,1,0:T(8,128)(2,1)} %broadcast_in_dim.14, s32[96]{0:T(128)S(1)} %fusion.117, bf16[96,128,128]{2,1,0:T(8,128)(2,1)} %param.8), kind=kCustom, calls=%fused_computation.9 | custom fusion | bytes 9437568 | tf_op jit(solution)/shard_map/scatter | solution.py:51
  38.1 6.1 all-to-all-start.1
  44.5 5.7 psum.91
  53.2 128.7 %all-to-all-done.1 = bf16[8,24,128,128]{3,2,1,0:T(8,128)(2,1)} async-done(((bf16[8,24,128,128]{3,2,1,0:T(8,128)(2,1)}), bf16[8,24,128,128]{3,2,1,0:T(8,128)(2,1)}, u32[]{:S(2)}, u32[]{:S(2)}) %all-to-all-start.1) | async-done | bytes 6291488 | tf_op jit(solution)/shard_map/all_to_all | solution.py:59
  181.9 5.6 fusion.48
  187.4 5.7 fusion.14
  194.9 35.2 %all-reduce.5.cloned.1.call-done = f32[64,4096]{1,0:T(8,128)} async-done(((f32[64,4096]{1,0:T(8,128)}), f32[64,4096]{1,0:T(8,128)}) %all-reduce.5.cloned.1.call-update) | async-done | bytes 1048592 | tf_op jit(solution)/shard_map/psum | solution.py:79
  231.5 21.5 %psum.93 = f32[64]{0:T(128)S(1)} all-reduce(f32[64]{0:T(128)S(1)} %multiply_reduce_fusion.7), channel_id=1, replica_groups=mesh['row'=4,'col'=8] {'col'}, use_global_device_ids=true, to_apply=%region_8.10 | all-reduce | flops 64 | bytes 512 | tf_op jit(solution)/shard_map/psum | solution.py:93
  254.7 2.7 gather_fusion.1
  257.4 8.1 fusion.51
  265.5 6.7 fusion.80
  274.7 121.8 %all-gather.5.cloned.1.call-done = f32[8,64,4096]{2,1,0:T(8,128)} async-done(((f32[1,64,4096]{2,1,0:T(8,128)}), f32[8,64,4096]{2,1,0:T(8,128)}) %all-gather.5.cloned.1.call-update) | async-done | bytes 8388624 | tf_op jit(solution)/shard_map/all_gather | solution.py:109
  396.5 5.0 reduce_sum.132
  404.0 6.4 psum.94
  411.8 2.7 gather_fusion.2
  414.5 5.6 fusion.54
  420.1 5.8 fusion.10
  427.6 34.1 %all-reduce.7.cloned.1.call-done = f32[64,4096]{1,0:T(8,128)} async-done(((f32[64,4096]{1,0:T(8,128)}), f32[64,4096]{1,0:T(8,128)}) %all-reduce.7.cloned.1.call-update) | async-done | bytes 1048592 | tf_op jit(solution)/shard_map/psum | solution.py:79
  463.2 21.8 %psum.96 = f32[64]{0:T(128)S(1)} all-reduce(f32[64]{0:T(128)S(1)} %multiply_reduce_fusion.5), channel_id=1, replica_groups=mesh['row'=4,'col'=8] {'col'}, use_global_device_ids=true, to_apply=%region_14.16 | all-reduce | flops 64 | bytes 512 | tf_op jit(solution)/shard_map/psum | solution.py:93
  486.7 2.7 gather_fusion.3
  489.4 8.1 fusion.57
  497.5 5.7 fusion.83
  504.5 121.8 %all-gather.7.cloned.1.call-done = f32[8,64,4096]{2,1,0:T(8,128)} async-done(((f32[1,64,4096]{2,1,0:T(8,128)}), f32[8,64,4096]{2,1,0:T(8,128)}) %all-gather.7.cloned.1.call-update) | async-done | bytes 8388624 | tf_op jit(solution)/shard_map/all_gather | solution.py:109
  626.3 5.0 reduce_sum.135
  633.8 6.3 psum.97
  641.6 2.7 gather_fusion.4
  644.3 5.6 fusion.60
  649.9 5.8 fusion.6
  657.3 34.1 %all-reduce.9.cloned.1.call-done = f32[64,4096]{1,0:T(8,128)} async-done(((f32[64,4096]{1,0:T(8,128)}), f32[64,4096]{1,0:T(8,128)}) %all-reduce.9.cloned.1.call-update) | async-done | bytes 1048592 | tf_op jit(solution)/shard_map/psum | solution.py:79
  693.0 21.6 %psum.99 = f32[64]{0:T(128)S(1)} all-reduce(f32[64]{0:T(128)S(1)} %multiply_reduce_fusion.3), channel_id=1, replica_groups=mesh['row'=4,'col'=8] {'col'}, use_global_device_ids=true, to_apply=%region_20.22 | all-reduce | flops 64 | bytes 512 | tf_op jit(solution)/shard_map/psum | solution.py:93
  717.2 2.7 gather_fusion.5
  719.9 8.1 fusion.63
  728.0 5.7 fusion.86
  735.0 121.8 %all-gather.9.cloned.1.call-done = f32[8,64,4096]{2,1,0:T(8,128)} async-done(((f32[1,64,4096]{2,1,0:T(8,128)}), f32[8,64,4096]{2,1,0:T(8,128)}) %all-gather.9.cloned.1.call-update) | async-done | bytes 8388624 | tf_op jit(solution)/shard_map/all_gather | solution.py:109
  856.7 5.0 reduce_sum.138
  864.3 6.6 psum.100
  875.0 5.6 fusion.66
  880.6 5.8 fusion.2
  888.1 34.1 %all-reduce.11.cloned.1.call-done = f32[64,4096]{1,0:T(8,128)} async-done(((f32[64,4096]{1,0:T(8,128)}), f32[64,4096]{1,0:T(8,128)}) %all-reduce.11.cloned.1.call-update) | async-done | bytes 1048592 | tf_op jit(solution)/shard_map/psum | solution.py:79
  923.7 21.5 %psum.102 = f32[64]{0:T(128)S(1)} all-reduce(f32[64]{0:T(128)S(1)} %multiply_reduce_fusion.1), channel_id=1, replica_groups=mesh['row'=4,'col'=8] {'col'}, use_global_device_ids=true, to_apply=%region_26.28 | all-reduce | flops 64 | bytes 512 | tf_op jit(solution)/shard_map/psum | solution.py:93
  947.9 2.7 gather_fusion.7
  950.6 8.1 fusion.69
  958.7 5.7 fusion.89
  965.7 121.8 %all-gather.11.cloned.1.call-done = f32[8,64,4096]{2,1,0:T(8,128)} async-done(((f32[1,64,4096]{2,1,0:T(8,128)}), f32[8,64,4096]{2,1,0:T(8,128)}) %all-gather.11.cloned.1.call-update) | async-done | bytes 8388624 | tf_op jit(solution)/shard_map/all_gather | solution.py:109
  1087.6 5.0 reduce_sum.141
  1094.2 6.2 psum.103
  (88 shorter events, 54.6 us)
Async XLA Ops:
  11.9 26.2 %all-to-all-start = ((s32[8,24,2]{1,2,0:T(2,128)}), s32[8,24,2]{1,2,0:T(2,128)S(1)}, u32[]{:S(2)}, u32[]{:S(2)}) async-start(s32[8,24,2]{1,2,0:T(2,128)} %copy.46), calls=%async_computation | async-start | bytes 16384 | tf_op jit(solution)/shard_map/all_to_all | solution.py:66
  38.1 6.2 copy-start.1
  38.1 143.8 %all-to-all-start.1 = ((bf16[8,24,128,128]{3,2,1,0:T(8,128)(2,1)}), bf16[8,24,128,128]{3,2,1,0:T(8,128)(2,1)}, u32[]{:S(2)}, u32[]{:S(2)}) async-start(bf16[8,24,128,128]{3,2,1,0:T(8,128)(2,1)} %bitcast.160), calls=%async_computation.1 | async-start | bytes 12582912 | tf_op jit(solution)/shard_map/all_to_all | solution.py:59
  44.2 185.9 %all-reduce.5.cloned.1.call-start = ((), (), s32[]{:S(2)}) async-start(), calls=%async_computation.2 | async-start | bytes 2097152 | tf_op jit(solution)/shard_map/psum | solution.py:79
  194.8 201.7 %all-gather.5.cloned.1.call-start = ((), (), s32[]{:S(2)}) async-start(), calls=%async_computation.3 | async-start | bytes 9437184 | tf_op jit(solution)/shard_map/all_gather | solution.py:109
  274.7 187.1 %all-reduce.7.cloned.1.call-start = ((), (), s32[]{:S(2)}) async-start(), calls=%async_computation.4 | async-start | bytes 2097152 | tf_op jit(solution)/shard_map/psum | solution.py:79
  427.6 198.7 %all-gather.7.cloned.1.call-start = ((), (), s32[]{:S(2)}) async-start(), calls=%async_computation.5 | async-start | bytes 9437184 | tf_op jit(solution)/shard_map/all_gather | solution.py:109
  504.4 126.8 %copy-start.4 = (f32[64,4096]{1,0:T(8,128)S(1)}, f32[64,4096]{1,0:T(8,128)}, u32[]{:S(2)}) copy-start(f32[64,4096]{1,0:T(8,128)} %get-tuple-element.25) | copy-start | bytes 3145732
  504.4 187.0 %all-reduce.9.cloned.1.call-start = ((), (), s32[]{:S(2)}) async-start(), calls=%async_computation.6 | async-start | bytes 2097152 | tf_op jit(solution)/shard_map/psum | solution.py:79
  657.3 199.5 %all-gather.9.cloned.1.call-start = ((), (), s32[]{:S(2)}) async-start(), calls=%async_computation.7 | async-start | bytes 9437184 | tf_op jit(solution)/shard_map/all_gather | solution.py:109
  734.9 126.8 %copy-start.3 = (f32[64,4096]{1,0:T(8,128)S(1)}, f32[64,4096]{1,0:T(8,128)}, u32[]{:S(2)}) copy-start(f32[64,4096]{1,0:T(8,128)} %get-tuple-element.21) | copy-start | bytes 3145732
  734.9 187.3 %all-reduce.11.cloned.1.call-start = ((), (), s32[]{:S(2)}) async-start(), calls=%async_computation.8 | async-start | bytes 2097152 | tf_op jit(solution)/shard_map/psum | solution.py:79
  886.4 35.8 %copy-start = (f32[64,4096]{1,0:T(8,128)S(1)}, f32[64,4096]{1,0:T(8,128)}, u32[]{:S(2)}) copy-start(f32[64,4096]{1,0:T(8,128)} %get-tuple-element.19) | copy-start | bytes 3145732
  888.0 199.6 %all-gather.11.cloned.1.call-start = ((), (), s32[]{:S(2)}) async-start(), calls=%async_computation.9 | async-start | bytes 9437184 | tf_op jit(solution)/shard_map/all_gather | solution.py:109
  965.7 126.9 %copy-start.2 = (f32[64,4096]{1,0:T(8,128)S(1)}, f32[64,4096]{1,0:T(8,128)}, u32[]{:S(2)}) copy-start(f32[64,4096]{1,0:T(8,128)} %get-tuple-element.17) | copy-start | bytes 3145732
Sparse Core Ops, SparseCore 0:
  195.0 35.1 all-reduce.4
  274.8 121.6 all-gather.4
  427.7 33.9 all-reduce.6
  504.5 121.6 all-gather.6
  657.4 33.9 all-reduce.8
  735.0 121.6 all-gather.8
  888.1 34.0 all-reduce.10
  965.8 121.6 all-gather.10
